TPU v7x, 256 devices: a whole 4x4x8 slice. The times are simulated.
256 devices in a mesh: ctx: 8 (over x, core), ch: 32 (over y, z).
Axes of the slice: x: 4, y: 4, z: 8, core: 2. Of those that a mesh axis runs over, the one named last changes fastest.
Arguments:
- tokens_in: bfloat16 [8192, 8192], P(('ctx', 'ch')), may hold values from -6 to 6
- norm_gain: float32 [8192], replicated, may hold values from 0.1 to 1.9
- proj_weight: bfloat16 [3, 8192, 8192], P(None, 'ctx', 'ch'), may hold values from -0.0625 to 0.0625
- conv_weight: float32 [3, 7, 8192], P(None, None, 'ch'), may hold values from -2 to 2
- decay_rate: float32 [16, 8192], P(None, 'ch'), may hold values from 6.1035157e-06 to 0.04
- residue: float32 [16, 8192], P(None, 'ch'), may hold values from -1.5 to 1.5
- skip_gain: float32 [8192], P('ch'), may hold values from -3 to 3
Outputs:
- gated: bfloat16 [8192, 8192], P(('ctx', 'ch'))
All inputs are finite; a program needn't handle non-finite values.
Results may differ from a plain program's by a relative error of at most 0.008.
Values may be sent and summed in bfloat16 or wider, within the bound.
No kernel may reach another device: no remote copies, remote signals or barrier semaphores. Data moves between devices by JAX's collectives and lax.ppermute only.
A program may use at most 128 MiB of HBM per device.

v0:
```python
import jax
import jax.numpy as jnp
from jax import lax
from jax.sharding import PartitionSpec as P

norm_eps = 1e-05


def shifted(shard, axis, by):
    length = lax.axis_size(axis)
    pairs = [(i, i + by) for i in range(length) if 0 <= i + by < length]
    return lax.ppermute(shard, axis, pairs)


def on_device(tokens_in, norm_gain, proj_weight, conv_weight, decay_rate, residue, skip_gain):
    widened = tokens_in.astype(jnp.float32)
    mean_square = jnp.mean(widened * widened, axis=-1, keepdims=True)
    normed = (widened * lax.rsqrt(mean_square + norm_eps) * norm_gain[None, :]).astype(jnp.bfloat16)
    gathered = lax.all_gather(normed, "ch", axis=0, tiled=True)
    row_count = gathered.shape[0]
    chan_count = proj_weight.shape[2]
    summed = jnp.einsum(
        "tf,ifc->itc",
        gathered,
        lax.all_gather(proj_weight, "ctx", axis=1, tiled=True),
        preferred_element_type=jnp.float32,
    )
    projected = summed.astype(jnp.bfloat16)
    tap_count = conv_weight.shape[1]
    reach = tap_count - 1
    rim_rows = shifted(projected[:, row_count - reach :, :], "ctx", 1)
    padded = jnp.concatenate([rim_rows, projected], axis=1).astype(jnp.float32)
    featured = jnp.zeros((3, row_count, chan_count), jnp.float32)
    for shift_idx in range(tap_count):
        featured = (
            featured
            + conv_weight[:, shift_idx, None, :]
            * padded[:, reach - shift_idx : reach - shift_idx + row_count, :]
        )
    queries = featured[0]
    mixed = featured[1] * featured[2]
    highest = lax.Precision.HIGHEST
    in_scale = jnp.sqrt(-jnp.expm1(-2.0 * decay_rate))
    span_rows = min(128, row_count)
    span_count = row_count // span_rows
    positions = jnp.arange(span_rows, dtype=jnp.float32)
    lag_decay = jnp.exp(-decay_rate[:, None, :] * positions[None, :, None])
    impulse = jnp.sum((residue * in_scale)[:, None, :] * lag_decay, axis=0)
    offsets = jnp.arange(span_rows)[:, None] - jnp.arange(span_rows)[None, :]
    lag_table = (offsets[None, :, :] == jnp.arange(span_rows)[:, None, None]).astype(jnp.float32)
    toeplitz = jnp.einsum("lc,lts->cts", impulse, lag_table, precision=highest)
    spans_in = mixed.reshape(span_count, span_rows, chan_count)
    inside = jnp.einsum("cts,jsc->jtc", toeplitz, spans_in, precision=highest)
    end_weight = in_scale[:, None, :] * jnp.exp(
        -decay_rate[:, None, :] * (span_rows - 1.0 - positions)[None, :, None]
    )
    span_ends = jnp.einsum("jsc,msc->jmc", spans_in, end_weight, precision=highest)
    span_decay = jnp.exp(-decay_rate * float(span_rows))

    def advance(carried, span_end):
        return (span_decay * carried + span_end, carried)

    zero_state = jnp.zeros(decay_rate.shape, jnp.float32)
    local_end, starts = lax.scan(advance, zero_state, span_ends)
    whole_decay = jnp.exp(-decay_rate * float(row_count))

    def handoff(unused_turn, incoming):
        return shifted(whole_decay * incoming + local_end, "ctx", 1)

    incoming = lax.fori_loop(0, lax.axis_size("ctx") - 1, handoff, zero_state)
    span_starts = jnp.arange(span_count, dtype=jnp.float32) * float(span_rows)
    starts = (
        starts
        + jnp.exp(-decay_rate[None, :, :] * span_starts[:, None, None]) * incoming[None, :, :]
    )
    out_weight = residue[:, None, :] * jnp.exp(
        -decay_rate[:, None, :] * (positions + 1.0)[None, :, None]
    )
    outside = jnp.einsum("jmc,mtc->jtc", starts, out_weight, precision=highest)
    filtered = (inside + outside).reshape(row_count, chan_count)
    gated = (queries * (filtered + skip_gain[None, :] * mixed)).astype(jnp.bfloat16)
    return lax.all_to_all(gated, "ch", split_axis=0, concat_axis=1, tiled=True)


def solution(mesh):
    in_specs = (
        P(("ctx", "ch"), None),
        P(),
        P(None, "ctx", "ch"),
        P(None, None, "ch"),
        P(None, "ch"),
        P(None, "ch"),
        P("ch"),
    )
    out_specs = P(("ctx", "ch"), None)
    return jax.shard_map(
        on_device, mesh=mesh, in_specs=in_specs, out_specs=out_specs, check_vma=False
    )
```

profile of v0, /device:TPU:34, one launch (start us, length us, event | category | flops | bytes accessed | tf_op | source)
XLA Modules:
  0.0 376.8 jit_solution(1986812862186608656)
XLA Ops:
  6.5 0.7 all-gather.5.cloned.1.call-update
  7.3 1.3 fusion.38
  8.6 2.0 fusion.40
  10.9 1.7 multiply_reduce_fusion
  12.7 9.6 %fusion.4 = f32[256,128,128]{2,0,1:T(8,128)} fusion(s32[128,128]{1,0:T(8,128)S(1)} %iota_subtract_fusion, f32[128,256]{0,1:T(8,128)S(1)} %multiply_reduce_fusion), kind=kOutput, calls=%fused_computation.8 | convolution fusion | flops 6444548096 | bytes 16973824 | tf_op jit(solution)/shard_map/lc,lts->cts/dot_general | solution.py:51
  22.2 58.8 %all-gather.5.cloned.1.call-done = bf16[3,8192,256]{2,1,0:T(8,128)(2,1)} async-done(((bf16[3,1024,256]{2,1,0:T(8,128)(2,1)}), bf16[3,8192,256]{2,1,0:T(8,128)(2,1)}) %all-gather.5.cloned.1.call-update) | async-done | bytes 12582928 | tf_op jit(solution)/shard_map/all_gather | solution.py:25
  81.0 141.5 %all-gather.3.cloned.1.call-done = bf16[1024,8192]{1,0:T(8,128)(2,1)} async-done(((bf16[32,8192]{1,0:T(8,128)(2,1)}), bf16[1024,8192]{1,0:T(8,128)(2,1)}) %all-gather.3.cloned.1.call-update) | async-done | bytes 16777232 | tf_op jit(solution)/shard_map/all_gather | solution.py:19
  222.6 18.7 %fusion.23 = bf16[3,1024,256]{2,1,0:T(8,128)(2,1)S(1)} fusion(bf16[3,8192,256]{2,1,0:T(8,128)(2,1)} %all-gather.5.cloned.1.call-done, bf16[1024,8192]{1,0:T(8,128)(2,1)} %all-gather.3.cloned.1.call-done), kind=kOutput, calls=%fused_computation.34 | convolution fusion | flops 12885688320 | bytes 30932992 | tf_op jit(solution)/shard_map/tf,ifc->itc/dot_general | solution.py:22
  241.3 2.1 collective-permute-start.1
  243.4 0.7 copy.31
  244.3 2.0 collective-permute-done.1
  246.3 0.3 maximum_convert_fusion
  246.6 2.6 fusion.6
  249.4 0.4 copy.29
  249.8 38.4 %fusion.32 = f32[8,128,256]{1,0,2:T(8,128)} fusion(f32[8,128,256]{1,0,2:T(8,128)S(1)} %copy.29, f32[256,128,128]{2,0,1:T(8,128)} %fusion.4), kind=kOutput, calls=%fused_computation.37 | convolution fusion | flops 402653184 | bytes 18874368 | tf_op jit(solution)/shard_map/cts,jsc->jtc/dot_general | solution.py:53
  288.2 5.2 %fusion.29 = f32[8,16,256]{1,0,2:T(8,128)} fusion(f32[8,128,256]{1,0,2:T(8,128)S(1)} %copy.29, f32[128]{0:T(128)S(1)} %iota_subtract_fusion.1, f32[16,256]{0,1:T(8,128)S(1)} %copy.32, f32[16,256]{0,1:T(8,128)S(1)} %copy.28), kind=kOutput, calls=%fused_computation.36 | convolution fusion | flops 51380224 | bytes 1212928 | tf_op jit(solution)/shard_map/jsc,msc->jmc/dot_general | solution.py:57
  293.4 1.6 copy.34
  295.0 4.9 %while.24 = (s32[]{:T(128)}, f32[16,256]{1,0:T(8,128)S(1)}, f32[8,16,256]{2,1,0:T(8,128)}, f32[16,256]{1,0:T(8,128)S(1)}, f32[8,16,256]{2,1,0:T(8,128)S(1)}, /*index=5*/s32[]{:T(128)}, s32[]{:T(128)}) while((s32[]{:T(128)}, f32[16,256]{1,0:T(8,128)S(1)}, f32[8,16,256]{2,1,0:T(8,128)}, f32[16,256]{1,0:T(8,128)S(1)}, ...), condition=%wide.region_3.4_spmd.clone, body=%wide.region_2.3_spmd.clone.sunk | while | flops 16387 | bytes 98408 | solution.py:64
  295.0 0.6 bitcast_dynamic-update-slice_fusion.2
  295.6 0.6 bitcast_dynamic-update-slice_fusion.2
  296.2 0.6 bitcast_dynamic-update-slice_fusion.2
  296.8 0.6 bitcast_dynamic-update-slice_fusion.2
  297.4 0.6 bitcast_dynamic-update-slice_fusion.2
  298.1 0.6 bitcast_dynamic-update-slice_fusion.2
  298.7 0.6 bitcast_dynamic-update-slice_fusion.2
  299.3 0.6 bitcast_dynamic-update-slice_fusion.2
  299.9 35.4 %while.23 = (s32[]{:T(128)}, f32[16,256]{1,0:T(8,128)S(1)}, f32[16,256]{1,0:T(8,128)S(1)}, f32[16,256]{1,0:T(8,128)S(1)}, s32[]{:T(128)}) while((s32[]{:T(128)}, f32[16,256]{1,0:T(8,128)S(1)}, f32[16,256]{1,0:T(8,128)S(1)}, f32[16,256]{1,0:T(8,128)S(1)}, s32[]{:T(128)}) %tuple.55), condition=%wide.region_5.6_spmd, body=%wide.region_4.5_spmd.sunk | while | flops 8194 | bytes 131173 | solution.py:70
  299.9 1.9 collective-permute-start
  301.9 3.1 collective-permute-done
  305.0 1.9 collective-permute-start
  306.9 3.1 collective-permute-done
  310.1 1.9 collective-permute-start
  312.0 3.1 collective-permute-done
  315.1 1.9 collective-permute-start
  317.0 3.1 collective-permute-done
  320.2 1.9 collective-permute-start
  322.1 3.1 collective-permute-done
  325.2 1.9 collective-permute-start
  327.1 3.1 collective-permute-done
  330.3 1.9 collective-permute-start
  332.2 3.1 collective-permute-done
  335.3 1.0 multiply_add_fusion.1
  336.3 1.3 copy.35
  337.7 5.0 %fusion.35 = f32[8,128,256]{1,0,2:T(8,128)} fusion(f32[8,128,256]{1,0,2:T(8,128)S(1)} %copy-done, f32[8,16,256]{1,0,2:T(8,128)} %copy.35, f32[128]{0:T(128)S(1)} %iota_add_fusion, f32[16,256]{0,1:T(8,128)} %copy.31, f32[16,256]{0,1:T(8,128)S(1)} %copy.28), kind=kOutput, calls=%fused_computation.38 | convolution fusion | flops 51642368 | bytes 2261504 | tf_op jit(solution)/shard_map/jmc,mtc->jtc/dot_general | solution.py:79
  342.6 1.6 copy.36
  344.2 0.4 multiply_convert_fusion
  344.6 24.5 %all_to_all.16 = bf16[32,32,256]{2,1,0:T(8,128)(2,1)S(1)} all-to-all(bf16[32,32,256]{2,1,0:T(8,128)(2,1)S(1)} %multiply_convert_fusion), channel_id=1, replica_groups=mesh['ctx'=8,'ch'=32] {'ch'}, dimensions={0} | all-to-all | bytes 1048576 | tf_op jit(solution)/shard_map/all_to_all | solution.py:82
  369.1 0.8 copy.45
  (47 shorter events, 0.8 us)
Async XLA Ops:
  6.5 4.1 %copy-start.3 = (f32[16,256]{1,0:T(8,128)S(1)}, f32[16,256]{1,0:T(8,128)}, u32[]{:S(2)}) copy-start(f32[16,256]{1,0:T(8,128)} %param.15) | copy-start | bytes 49156
  6.5 4.1 %copy-start.1 = (f32[16,256]{1,0:T(8,128)S(1)}, f32[16,256]{1,0:T(8,128)}, u32[]{:S(2)}) copy-start(f32[16,256]{1,0:T(8,128)} %param.16) | copy-start | bytes 49156
  6.5 6.1 %copy-start.2 = (f32[3,7,256]{2,1,0:T(8,128)S(1)}, f32[3,7,256]{2,1,0:T(8,128)}, u32[]{:S(2)}) copy-start(f32[3,7,256]{2,1,0:T(8,128)} %param.14) | copy-start | bytes 64516
  6.5 74.5 %all-gather.5.cloned.1.call-start = ((), (), s32[]{:S(2)}) async-start(), calls=%async_computation.2 | async-start | bytes 14155776 | tf_op jit(solution)/shard_map/all_gather | solution.py:25
  7.3 215.3 %all-gather.3.cloned.1.call-start = ((), (), s32[]{:S(2)}) async-start(), calls=%async_computation.1 | async-start | bytes 17301504 | tf_op jit(solution)/shard_map/all_gather | solution.py:19
  241.3 5.0 %collective-permute-start.1 = (bf16[3,6,256]{2,1,0:T(8,128)(2,1)S(1)}, bf16[3,6,256]{2,1,0:T(8,128)(2,1)S(1)}, u32[]{:S(2)}, u32[]{:S(2)}) collective-permute-start(bf16[3,6,256]{2,1,0:T(8,128)(2,1)S(1)} %slice.72), channel_id=1, source_target_pairs={{0,32},{32,64},{64,96},{96,128},{128,160},{160,192},{192,224},{1,3... | collective-permute-start | bytes 27656 | tf_op jit(solution)/shard_map/ppermute | solution.py:12
  293.4 44.3 %copy-start = (f32[8,128,256]{1,0,2:T(8,128)S(1)}, f32[8,128,256]{1,0,2:T(8,128)}, u32[]{:S(2)}) copy-start(f32[8,128,256]{1,0,2:T(8,128)} %fusion.32) | copy-start | bytes 3145732
  299.9 5.1 %collective-permute-start = (f32[16,256]{1,0:T(8,128)S(1)}, f32[16,256]{1,0:T(8,128)S(1)}, u32[]{:S(2)}, u32[]{:S(2)}) collective-permute-start(f32[16,256]{1,0:T(8,128)S(1)} %multiply_add_fusion.3), channel_id=1, source_target_pairs={{0,32},{32,64},{64,96},{96,128},{128,160},{160,192},{192,224},{1,3... | collective-permute-start | bytes 49160 | tf_op jit(solution)/shard_map/while/body/eval_jaxpr/ppermute | solution.py:12
  305.0 5.0 %collective-permute-start = (f32[16,256]{1,0:T(8,128)S(1)}, f32[16,256]{1,0:T(8,128)S(1)}, u32[]{:S(2)}, u32[]{:S(2)}) collective-permute-start(f32[16,256]{1,0:T(8,128)S(1)} %multiply_add_fusion.3), channel_id=1, source_target_pairs={{0,32},{32,64},{64,96},{96,128},{128,160},{160,192},{192,224},{1,3... | collective-permute-start | bytes 49160 | tf_op jit(solution)/shard_map/while/body/eval_jaxpr/ppermute | solution.py:12
  310.1 5.0 %collective-permute-start = (f32[16,256]{1,0:T(8,128)S(1)}, f32[16,256]{1,0:T(8,128)S(1)}, u32[]{:S(2)}, u32[]{:S(2)}) collective-permute-start(f32[16,256]{1,0:T(8,128)S(1)} %multiply_add_fusion.3), channel_id=1, source_target_pairs={{0,32},{32,64},{64,96},{96,128},{128,160},{160,192},{192,224},{1,3... | collective-permute-start | bytes 49160 | tf_op jit(solution)/shard_map/while/body/eval_jaxpr/ppermute | solution.py:12
  315.1 5.0 %collective-permute-start = (f32[16,256]{1,0:T(8,128)S(1)}, f32[16,256]{1,0:T(8,128)S(1)}, u32[]{:S(2)}, u32[]{:S(2)}) collective-permute-start(f32[16,256]{1,0:T(8,128)S(1)} %multiply_add_fusion.3), channel_id=1, source_target_pairs={{0,32},{32,64},{64,96},{96,128},{128,160},{160,192},{192,224},{1,3... | collective-permute-start | bytes 49160 | tf_op jit(solution)/shard_map/while/body/eval_jaxpr/ppermute | solution.py:12
  320.2 5.0 %collective-permute-start = (f32[16,256]{1,0:T(8,128)S(1)}, f32[16,256]{1,0:T(8,128)S(1)}, u32[]{:S(2)}, u32[]{:S(2)}) collective-permute-start(f32[16,256]{1,0:T(8,128)S(1)} %multiply_add_fusion.3), channel_id=1, source_target_pairs={{0,32},{32,64},{64,96},{96,128},{128,160},{160,192},{192,224},{1,3... | collective-permute-start | bytes 49160 | tf_op jit(solution)/shard_map/while/body/eval_jaxpr/ppermute | solution.py:12
  325.2 5.0 %collective-permute-start = (f32[16,256]{1,0:T(8,128)S(1)}, f32[16,256]{1,0:T(8,128)S(1)}, u32[]{:S(2)}, u32[]{:S(2)}) collective-permute-start(f32[16,256]{1,0:T(8,128)S(1)} %multiply_add_fusion.3), channel_id=1, source_target_pairs={{0,32},{32,64},{64,96},{96,128},{128,160},{160,192},{192,224},{1,3... | collective-permute-start | bytes 49160 | tf_op jit(solution)/shard_map/while/body/eval_jaxpr/ppermute | solution.py:12
  330.3 5.0 %collective-permute-start = (f32[16,256]{1,0:T(8,128)S(1)}, f32[16,256]{1,0:T(8,128)S(1)}, u32[]{:S(2)}, u32[]{:S(2)}) collective-permute-start(f32[16,256]{1,0:T(8,128)S(1)} %multiply_add_fusion.3), channel_id=1, source_target_pairs={{0,32},{32,64},{64,96},{96,128},{128,160},{160,192},{192,224},{1,3... | collective-permute-start | bytes 49160 | tf_op jit(solution)/shard_map/while/body/eval_jaxpr/ppermute | solution.py:12
  337.7 6.5 %copy-start.4 = (f32[256]{0:T(256)S(1)}, f32[256]{0:T(256)}, u32[]{:S(2)}) copy-start(f32[256]{0:T(256)} %param.17) | copy-start | bytes 3076
Sparse Core Ops, SparseCore 0:
  9.2 71.7 all-gather.4
  83.6 138.9 all-gather.2
where the time goes:
time: 377 us
  waiting for transfers between devices  225 us (60%)
  matrix products  76.7 us (20%)
  blocking collectives  24.5 us (6%)
  starting transfers between devices  15.5 us (4%)
  other arithmetic  14.5 us (4%)
  between operations  13.6 us (4%)
  local copies, waits for them, and re-layouts  6.84 us (2%)
    all_gather x1, waiting for transfers between devices, on_device(): gathered = lax.all_gather(normed, 'ch', axis=0, tiled=True)  142 us
    all_gather x1, waiting for transfers between devices, on_device(): lax.all_gather(proj_weight, 'ctx', axis=1, tiled=True)  58.8 us
    dot_general x1, matrix products, on_device(): inside = jnp.einsum('cts,jsc->jtc', toeplitz, spans_in, precision=highest)  38.4 us
    all_to_all x1, blocking collectives, on_device(): return lax.all_to_all(gated, 'ch', split_axis=0, concat_axis=1, tiled=True)  24.5 us
    ppermute x8, waiting for transfers between devices, shifted(): return lax.ppermute(shard, axis, pairs)  23.9 us
    dot_general x1, matrix products, on_device(): jnp.einsum('tf,ifc->itc', gathered, lax.all_gather(proj_weight, 'ctx', ax...  18.7 us
    ppermute x8, starting transfers between devices, shifted(): return lax.ppermute(shard, axis, pairs)  15.5 us
    dot_general x1, matrix products, on_device(): toeplitz = jnp.einsum('lc,lts->cts', impulse, lag_table, precision=highest)  9.55 us
  transfers between devices with their start and end apart: 10, of which 10 were waited for; matrix products, arithmetic and copies ran while one was open for 4% of the time, Pallas kernels for 0%

commit v1 on v0

--- a/solution.py
+++ b/solution.py
@@ -4,6 +4,13 @@
 from jax.sharding import PartitionSpec as P
 
 norm_eps = 1e-05
+
+
+def swap_blocks(x, mesh_axis, split, join):
+    peers = lax.axis_size(mesh_axis)
+    blocks = jnp.stack(jnp.split(x, peers, axis=split), axis=0)
+    blocks = lax.all_to_all(blocks, mesh_axis, split_axis=0, concat_axis=0)
+    return jnp.concatenate(blocks, axis=join)
 
 
 def shifted(shard, axis, by):
@@ -79,7 +86,7 @@
     outside = jnp.einsum("jmc,mtc->jtc", starts, out_weight, precision=highest)
     filtered = (inside + outside).reshape(row_count, chan_count)
     gated = (queries * (filtered + skip_gain[None, :] * mixed)).astype(jnp.bfloat16)
-    return lax.all_to_all(gated, "ch", split_axis=0, concat_axis=1, tiled=True)
+    return swap_blocks(gated, "ch", 0, 1)
 
 
 def solution(mesh):

time: 377 us -> 383 us (1.016)
  no operation moved by 1% of the time
where the time goes in v1:
time: 383 us
  waiting for transfers between devices  225 us (59%)
  matrix products  77.1 us (20%)
  blocking collectives  24.5 us (6%)
  other arithmetic  16.5 us (4%)
  starting transfers between devices  15.5 us (4%)
  between operations  13.8 us (4%)
  local copies, waits for them, and re-layouts  10 us (3%)
    all_gather x1, waiting for transfers between devices, on_device(): gathered = lax.all_gather(normed, 'ch', axis=0, tiled=True)  142 us
    all_gather x1, waiting for transfers between devices, on_device(): lax.all_gather(proj_weight, 'ctx', axis=1, tiled=True)  58.8 us
    dot_general x1, matrix products, on_device(): inside = jnp.einsum('cts,jsc->jtc', toeplitz, spans_in, precision=highest)  38.8 us
    all_to_all x1, blocking collectives, swap_blocks(): blocks = lax.all_to_all(blocks, mesh_axis, split_axis=0, concat_axis=0)  24.5 us
    ppermute x8, waiting for transfers between devices, shifted(): return lax.ppermute(shard, axis, pairs)  23.9 us
    dot_general x1, matrix products, on_device(): jnp.einsum('tf,ifc->itc', gathered, lax.all_gather(proj_weight, 'ctx', ax...  18.7 us
    ppermute x8, starting transfers between devices, shifted(): return lax.ppermute(shard, axis, pairs)  15.5 us
    dot_general x1, matrix products, on_device(): toeplitz = jnp.einsum('lc,lts->cts', impulse, lag_table, precision=highest)  9.55 us
  transfers between devices with their start and end apart: 10, of which 10 were waited for; matrix products, arithmetic and copies ran while one was open for 4% of the time, Pallas kernels for 0%

profile of v1, /device:TPU:34, one launch (start us, length us, event | category | flops | bytes accessed | tf_op | source)
XLA Modules:
  0.0 382.5 jit_solution(1816211882507729699)
XLA Ops:
  6.5 0.7 all-gather.5.cloned.1.call-update
  7.3 1.3 fusion.38
  8.6 2.0 fusion.40
  10.9 1.7 multiply_reduce_fusion
  12.7 9.6 %fusion.4 = f32[256,128,128]{2,0,1:T(8,128)} fusion(s32[128,128]{1,0:T(8,128)S(1)} %iota_subtract_fusion, f32[128,256]{0,1:T(8,128)S(1)} %multiply_reduce_fusion), kind=kOutput, calls=%fused_computation.8 | convolution fusion | flops 6444548096 | bytes 16973824 | tf_op jit(solution)/shard_map/lc,lts->cts/dot_general | solution.py:58
  22.2 58.8 %all-gather.5.cloned.1.call-done = bf16[3,8192,256]{2,1,0:T(8,128)(2,1)} async-done(((bf16[3,1024,256]{2,1,0:T(8,128)(2,1)}), bf16[3,8192,256]{2,1,0:T(8,128)(2,1)}) %all-gather.5.cloned.1.call-update) | async-done | bytes 12582928 | tf_op jit(solution)/shard_map/all_gather | solution.py:32
  81.0 141.5 %all-gather.3.cloned.1.call-done = bf16[1024,8192]{1,0:T(8,128)(2,1)} async-done(((bf16[32,8192]{1,0:T(8,128)(2,1)}), bf16[1024,8192]{1,0:T(8,128)(2,1)}) %all-gather.3.cloned.1.call-update) | async-done | bytes 16777232 | tf_op jit(solution)/shard_map/all_gather | solution.py:26
  222.6 18.7 %fusion.23 = bf16[3,1024,256]{2,1,0:T(8,128)(2,1)S(1)} fusion(bf16[3,8192,256]{2,1,0:T(8,128)(2,1)} %all-gather.5.cloned.1.call-done, bf16[1024,8192]{1,0:T(8,128)(2,1)} %all-gather.3.cloned.1.call-done), kind=kOutput, calls=%fused_computation.34 | convolution fusion | flops 12885688320 | bytes 30932992 | tf_op jit(solution)/shard_map/tf,ifc->itc/dot_general | solution.py:29
  241.3 2.1 collective-permute-start.1
  243.4 0.8 copy.31
  244.3 2.0 collective-permute-done.1
  246.6 2.6 fusion.6
  249.2 1.1 slice_multiply_fusion.7
  250.3 2.6 copy.29
  252.9 38.8 %fusion.32 = f32[8,128,256]{1,0,2:T(8,128)} fusion(f32[8,128,256]{1,0,2:T(8,128)} %copy.29, f32[256,128,128]{2,0,1:T(8,128)} %fusion.4), kind=kOutput, calls=%fused_computation.37 | convolution fusion | flops 402653184 | bytes 18874368 | tf_op jit(solution)/shard_map/cts,jsc->jtc/dot_general | solution.py:60
  291.7 5.2 %fusion.29 = f32[8,16,256]{1,0,2:T(8,128)} fusion(f32[8,128,256]{1,0,2:T(8,128)S(1)} %copy-done, f32[128]{0:T(128)S(1)} %iota_subtract_fusion.1, f32[16,256]{0,1:T(8,128)S(1)} %copy.32, f32[16,256]{0,1:T(8,128)S(1)} %copy.28), kind=kOutput, calls=%fused_computation.36 | convolution fusion | flops 51380224 | bytes 1212928 | tf_op jit(solution)/shard_map/jsc,msc->jmc/dot_general | solution.py:64
  296.8 1.5 copy.34
  298.4 4.9 %while.24 = (s32[]{:T(128)}, f32[16,256]{1,0:T(8,128)S(1)}, f32[8,16,256]{2,1,0:T(8,128)}, f32[16,256]{1,0:T(8,128)S(1)}, f32[8,16,256]{2,1,0:T(8,128)S(1)}, /*index=5*/s32[]{:T(128)}, s32[]{:T(128)}) while((s32[]{:T(128)}, f32[16,256]{1,0:T(8,128)S(1)}, f32[8,16,256]{2,1,0:T(8,128)}, f32[16,256]{1,0:T(8,128)S(1)}, ...), condition=%wide.region_3.4_spmd.clone, body=%wide.region_2.3_spmd.clone.sunk | while | flops 16387 | bytes 98408 | solution.py:71
  298.4 0.6 bitcast_dynamic-update-slice_fusion.2
  299.0 0.6 bitcast_dynamic-update-slice_fusion.2
  299.6 0.6 bitcast_dynamic-update-slice_fusion.2
  300.2 0.6 bitcast_dynamic-update-slice_fusion.2
  300.8 0.6 bitcast_dynamic-update-slice_fusion.2
  301.5 0.6 bitcast_dynamic-update-slice_fusion.2
  302.1 0.6 bitcast_dynamic-update-slice_fusion.2
  302.7 0.6 bitcast_dynamic-update-slice_fusion.2
  303.3 35.4 %while.23 = (s32[]{:T(128)}, f32[16,256]{1,0:T(8,128)S(1)}, f32[16,256]{1,0:T(8,128)S(1)}, f32[16,256]{1,0:T(8,128)S(1)}, s32[]{:T(128)}) while((s32[]{:T(128)}, f32[16,256]{1,0:T(8,128)S(1)}, f32[16,256]{1,0:T(8,128)S(1)}, f32[16,256]{1,0:T(8,128)S(1)}, s32[]{:T(128)}) %tuple.54), condition=%wide.region_5.6_spmd, body=%wide.region_4.5_spmd.sunk | while | flops 8194 | bytes 131173 | solution.py:77
  303.3 1.9 collective-permute-start
  305.3 3.1 collective-permute-done
  308.4 1.9 collective-permute-start
  310.3 3.1 collective-permute-done
  313.5 1.9 collective-permute-start
  315.4 3.1 collective-permute-done
  318.5 1.9 collective-permute-start
  320.4 3.1 collective-permute-done
  323.6 1.9 collective-permute-start
  325.5 3.1 collective-permute-done
  328.6 1.9 collective-permute-start
  330.5 3.1 collective-permute-done
  333.7 1.9 collective-permute-start
  335.6 3.1 collective-permute-done
  338.7 1.0 multiply_add_fusion.1
  339.7 1.3 copy.35
  341.0 4.9 %fusion.35 = f32[8,128,256]{1,0,2:T(8,128)} fusion(f32[8,128,256]{1,0,2:T(8,128)} %fusion.32, f32[8,16,256]{1,0,2:T(8,128)} %copy.35, f32[128]{0:T(128)S(1)} %iota_add_fusion, f32[16,256]{0,1:T(8,128)} %copy.31, f32[16,256]{0,1:T(8,128)S(1)} %copy.28), kind=kOutput, calls=%fused_computation.38 | convolution fusion | flops 51642368 | bytes 2261504 | tf_op jit(solution)/shard_map/jmc,mtc->jtc/dot_general | solution.py:86
  345.9 2.5 copy.36
  348.5 1.5 fusion.42
  350.3 24.5 %all_to_all.5 = bf16[32,32,256]{2,1,0:T(8,128)(2,1)S(1)} all-to-all(bf16[32,32,256]{2,1,0:T(8,128)(2,1)S(1)} %constant_dynamic-update-slice_fusion), channel_id=1, replica_groups=mesh['ctx'=8,'ch'=32] {'ch'}, dimensions={0} | all-to-all | bytes 1048576 | tf_op jit(solution)/shard_map/all_to_all | solution.py:12
  374.9 0.8 copy.45
  (79 shorter events, 1.0 us)
Async XLA Ops:
  6.5 4.1 %copy-start.3 = (f32[16,256]{1,0:T(8,128)S(1)}, f32[16,256]{1,0:T(8,128)}, u32[]{:S(2)}) copy-start(f32[16,256]{1,0:T(8,128)} %param.15) | copy-start | bytes 49156
  6.5 4.1 %copy-start.1 = (f32[16,256]{1,0:T(8,128)S(1)}, f32[16,256]{1,0:T(8,128)}, u32[]{:S(2)}) copy-start(f32[16,256]{1,0:T(8,128)} %param.16) | copy-start | bytes 49156
  6.5 6.1 %copy-start.2 = (f32[3,7,256]{2,1,0:T(8,128)S(1)}, f32[3,7,256]{2,1,0:T(8,128)}, u32[]{:S(2)}) copy-start(f32[3,7,256]{2,1,0:T(8,128)} %param.14) | copy-start | bytes 64516
  6.5 74.5 %all-gather.5.cloned.1.call-start = ((), (), s32[]{:S(2)}) async-start(), calls=%async_computation.2 | async-start | bytes 14155776 | tf_op jit(solution)/shard_map/all_gather | solution.py:32
  7.3 215.3 %all-gather.3.cloned.1.call-start = ((), (), s32[]{:S(2)}) async-start(), calls=%async_computation.1 | async-start | bytes 17301504 | tf_op jit(solution)/shard_map/all_gather | solution.py:26
  241.3 5.0 %collective-permute-start.1 = (bf16[3,6,256]{2,1,0:T(8,128)(2,1)S(1)}, bf16[3,6,256]{2,1,0:T(8,128)(2,1)S(1)}, u32[]{:S(2)}, u32[]{:S(2)}) collective-permute-start(bf16[3,6,256]{2,1,0:T(8,128)(2,1)S(1)} %slice.72), channel_id=1, source_target_pairs={{0,32},{32,64},{64,96},{96,128},{128,160},{160,192},{192,224},{1,3... | collective-permute-start | bytes 27656 | tf_op jit(solution)/shard_map/ppermute | solution.py:19
  252.9 38.8 %copy-start = (f32[8,128,256]{1,0,2:T(8,128)S(1)}, f32[8,128,256]{1,0,2:T(8,128)}, u32[]{:S(2)}) copy-start(f32[8,128,256]{1,0,2:T(8,128)} %copy.29) | copy-start | bytes 3145732
  303.3 5.1 %collective-permute-start = (f32[16,256]{1,0:T(8,128)S(1)}, f32[16,256]{1,0:T(8,128)S(1)}, u32[]{:S(2)}, u32[]{:S(2)}) collective-permute-start(f32[16,256]{1,0:T(8,128)S(1)} %multiply_add_fusion.3), channel_id=1, source_target_pairs={{0,32},{32,64},{64,96},{96,128},{128,160},{160,192},{192,224},{1,3... | collective-permute-start | bytes 49160 | tf_op jit(solution)/shard_map/while/body/eval_jaxpr/ppermute | solution.py:19
  308.4 5.0 %collective-permute-start = (f32[16,256]{1,0:T(8,128)S(1)}, f32[16,256]{1,0:T(8,128)S(1)}, u32[]{:S(2)}, u32[]{:S(2)}) collective-permute-start(f32[16,256]{1,0:T(8,128)S(1)} %multiply_add_fusion.3), channel_id=1, source_target_pairs={{0,32},{32,64},{64,96},{96,128},{128,160},{160,192},{192,224},{1,3... | collective-permute-start | bytes 49160 | tf_op jit(solution)/shard_map/while/body/eval_jaxpr/ppermute | solution.py:19
  313.5 5.0 %collective-permute-start = (f32[16,256]{1,0:T(8,128)S(1)}, f32[16,256]{1,0:T(8,128)S(1)}, u32[]{:S(2)}, u32[]{:S(2)}) collective-permute-start(f32[16,256]{1,0:T(8,128)S(1)} %multiply_add_fusion.3), channel_id=1, source_target_pairs={{0,32},{32,64},{64,96},{96,128},{128,160},{160,192},{192,224},{1,3... | collective-permute-start | bytes 49160 | tf_op jit(solution)/shard_map/while/body/eval_jaxpr/ppermute | solution.py:19
  318.5 5.0 %collective-permute-start = (f32[16,256]{1,0:T(8,128)S(1)}, f32[16,256]{1,0:T(8,128)S(1)}, u32[]{:S(2)}, u32[]{:S(2)}) collective-permute-start(f32[16,256]{1,0:T(8,128)S(1)} %multiply_add_fusion.3), channel_id=1, source_target_pairs={{0,32},{32,64},{64,96},{96,128},{128,160},{160,192},{192,224},{1,3... | collective-permute-start | bytes 49160 | tf_op jit(solution)/shard_map/while/body/eval_jaxpr/ppermute | solution.py:19
  323.6 5.0 %collective-permute-start = (f32[16,256]{1,0:T(8,128)S(1)}, f32[16,256]{1,0:T(8,128)S(1)}, u32[]{:S(2)}, u32[]{:S(2)}) collective-permute-start(f32[16,256]{1,0:T(8,128)S(1)} %multiply_add_fusion.3), channel_id=1, source_target_pairs={{0,32},{32,64},{64,96},{96,128},{128,160},{160,192},{192,224},{1,3... | collective-permute-start | bytes 49160 | tf_op jit(solution)/shard_map/while/body/eval_jaxpr/ppermute | solution.py:19
  328.6 5.0 %collective-permute-start = (f32[16,256]{1,0:T(8,128)S(1)}, f32[16,256]{1,0:T(8,128)S(1)}, u32[]{:S(2)}, u32[]{:S(2)}) collective-permute-start(f32[16,256]{1,0:T(8,128)S(1)} %multiply_add_fusion.3), channel_id=1, source_target_pairs={{0,32},{32,64},{64,96},{96,128},{128,160},{160,192},{192,224},{1,3... | collective-permute-start | bytes 49160 | tf_op jit(solution)/shard_map/while/body/eval_jaxpr/ppermute | solution.py:19
  333.7 5.0 %collective-permute-start = (f32[16,256]{1,0:T(8,128)S(1)}, f32[16,256]{1,0:T(8,128)S(1)}, u32[]{:S(2)}, u32[]{:S(2)}) collective-permute-start(f32[16,256]{1,0:T(8,128)S(1)} %multiply_add_fusion.3), channel_id=1, source_target_pairs={{0,32},{32,64},{64,96},{96,128},{128,160},{160,192},{192,224},{1,3... | collective-permute-start | bytes 49160 | tf_op jit(solution)/shard_map/while/body/eval_jaxpr/ppermute | solution.py:19
  341.0 7.4 %copy-start.4 = (f32[256]{0:T(256)S(1)}, f32[256]{0:T(256)}, u32[]{:S(2)}) copy-start(f32[256]{0:T(256)} %param.17) | copy-start | bytes 3076
Sparse Core Ops, SparseCore 0:
  9.2 71.7 all-gather.4
  83.6 138.9 all-gather.2
